TPU v7x, 32 devices: a whole 2x2x4 slice. The times are simulated.
32 devices in a mesh: wide: 16 (over z, y, x), narrow: 2 (over core).
Axes of the slice: x: 2, y: 2, z: 4, core: 2. Of those that a mesh axis runs over, the one named last changes fastest.
Arguments:
- sample_t: float32 [512, 65536], P(('wide', 'narrow')), may hold values from -300 to 300
Outputs:
- basis: float32 [65536, 512], P(('wide', 'narrow'))
- factor_out: float32 [512, 512], replicated
All inputs are finite; a program needn't handle non-finite values.
Results may differ from a plain program's by a relative error of at most 0.000084.
Values sent between devices are 32-bit elements; how exact they have to be, the bound alone decides.
No kernel may reach another device: no remote copies, remote signals or barrier semaphores. Data moves between devices by JAX's collectives and lax.ppermute only.
A program may use at most 64 MiB of HBM per device.

v0:
```python
import math
import jax
import jax.numpy as jnp
from jax import lax
from jax.sharding import PartitionSpec as P

AXES = ("wide", "narrow")


def _mm(a, b):
    return jnp.dot(a, b, precision=lax.Precision.HIGHEST, preferred_element_type=jnp.float32)


def _diag_pair(block):
    lower = lax.linalg.cholesky(block)
    identity = jnp.eye(block.shape[0], dtype=block.dtype)
    solved = lax.linalg.triangular_solve(lower, identity, left_side=True, lower=True)
    return (lower, solved)


def factor_pair(matrix, b=128):
    n = matrix.shape[0]
    nb = n // b
    trail = matrix
    l_blk = {}
    d_inv = []
    for k in range(nb):
        l_kk, i_kk = _diag_pair(trail[:b, :b])
        d_inv.append(i_kk)
        l_blk[k, k] = l_kk
        if k < nb - 1:
            panel = _mm(trail[b:, :b], i_kk.T)
            for i in range(k + 1, nb):
                l_blk[i, k] = panel[(i - k - 1) * b : (i - k) * b]
            trail = trail[b:, b:] - _mm(panel, panel.T)
    inv = {}
    for j in range(nb):
        inv[j, j] = d_inv[j]
        for i in range(j + 1, nb):
            acc = _mm(l_blk[i, j], inv[j, j])
            for m in range(j + 1, i):
                acc = acc + _mm(l_blk[i, m], inv[m, j])
            inv[i, j] = -_mm(d_inv[i], acc)
    zero = jnp.zeros((b, b), matrix.dtype)
    lower = jnp.concatenate(
        [jnp.concatenate([l_blk.get((i, j), zero) for j in range(nb)], 1) for i in range(nb)], 0
    )
    lower_inv = jnp.concatenate(
        [jnp.concatenate([inv.get((i, j), zero) for j in range(nb)], 1) for i in range(nb)], 0
    )
    return (lower, lower_inv)


def _pair(count, bit):
    return [(i, i ^ bit) for i in range(count)]


def sum_by_halving(local, count):
    steps = count.bit_length() - 1
    assert 1 << steps == count and local.shape[0] % count == 0
    idx = lax.axis_index(AXES)
    buf = local
    for k in range(steps):
        half = buf.shape[0] // 2
        b = idx >> k & 1
        keep = lax.dynamic_slice_in_dim(buf, b * half, half, 0)
        send = lax.dynamic_slice_in_dim(buf, (1 - b) * half, half, 0)
        buf = keep + lax.ppermute(send, AXES, _pair(count, 1 << k))
    for k in reversed(range(steps)):
        b = idx >> k & 1
        recv = lax.ppermute(buf, AXES, _pair(count, 1 << k))
        lo = jnp.where(b == 0, buf, recv)
        hi = jnp.where(b == 0, recv, buf)
        buf = jnp.concatenate([lo, hi], 0)
    return buf


def per_device(sample_t):
    wide_count = lax.axis_size("wide")
    narrow_count = lax.axis_size("narrow")
    count = wide_count * narrow_count
    rows_t = lax.all_to_all(sample_t, AXES, split_axis=1, concat_axis=0, tiled=True)
    gram_local = jnp.dot(
        rows_t, rows_t.T, precision=lax.Precision.HIGHEST, preferred_element_type=jnp.float32
    )
    gram_total = sum_by_halving(gram_local, count)
    lower, lower_inv = factor_pair(gram_total)
    upper_factor = lower.T
    inverse = lower_inv.T
    total_rows = rows_t.shape[1] * count
    scale_root = math.sqrt(total_rows)
    product = lax.dot_general(
        rows_t,
        inverse,
        (((0,), (0,)), ((), ())),
        precision=lax.Precision.HIGHEST,
        preferred_element_type=jnp.float32,
    )
    return (product * scale_root, upper_factor / scale_root)


def solution(mesh):
    in_specs = (P(AXES, None),)
    out_specs = (P(AXES, None), P())
    return jax.shard_map(
        per_device, mesh=mesh, in_specs=in_specs, out_specs=out_specs, check_vma=False
    )
```

profile of v0, /device:TPU:0, one launch (start us, length us, event | category | flops | bytes accessed | tf_op | source)
XLA Modules:
  0.0 287.7 jit_solution(4122485212012799821)
XLA Ops:
  0.6 4.7 %copy.140 = f32[2,32,8,2048]{3,2,0,1:T(8,128)} copy(f32[2,32,8,2048]{3,2,1,0:T(8,128)} %bitcast.83) | data formatting | bytes 8388608 | tf_op jit(solution)/shard_map/all_to_all | solution.py:82
  5.3 7.4 %all-to-all-start = ((f32[16,32,2048]{2,0,1:T(8,128)}), f32[16,32,2048]{2,0,1:T(8,128)}, u32[]{:S(2)}, u32[]{:S(2)}) async-start(f32[16,32,2048]{2,0,1:T(8,128)} %bitcast.82), calls=%async_computation | async-start | bytes 8388608 | tf_op jit(solution)/shard_map/all_to_all | solution.py:82
  12.8 93.9 %all-to-all-done = f32[16,32,2048]{2,0,1:T(8,128)} async-done(((f32[16,32,2048]{2,0,1:T(8,128)}), f32[16,32,2048]{2,0,1:T(8,128)}, u32[]{:S(2)}, u32[]{:S(2)}) %all-to-all-start) | async-done | bytes 4194336 | tf_op jit(solution)/shard_map/all_to_all | solution.py:82
  106.6 9.8 %fusion.71 = f32[512,512]{1,0:T(8,128)S(1)} fusion(f32[512,2048]{1,0:T(8,128)} %bitcast.1), kind=kOutput, calls=%fused_computation.137 | convolution fusion | flops 6442450944 | bytes 5242880 | tf_op jit(solution)/shard_map/dot_general | solution.py:83
  116.6 1.9 collective-permute-done
  118.6 1.3 collective-permute-start.1
  119.9 7.1 %collective-permute-done.1 = f32[128,512]{1,0:T(8,128)S(1)} collective-permute-done((f32[128,512]{1,0:T(8,128)S(1)}, f32[128,512]{1,0:T(8,128)S(1)}, u32[]{:S(2)}, u32[]{:S(2)}) %collective-permute-start.1) | collective-permute-done | bytes 262176 | tf_op jit(solution)/shard_map/ppermute | solution.py:68
  127.0 1.3 collective-permute-start.2
  128.3 3.7 %collective-permute-done.2 = f32[64,512]{1,0:T(8,128)S(1)} collective-permute-done((f32[64,512]{1,0:T(8,128)S(1)}, f32[64,512]{1,0:T(8,128)S(1)}, u32[]{:S(2)}, u32[]{:S(2)}) %collective-permute-start.2) | collective-permute-done | bytes 131104 | tf_op jit(solution)/shard_map/ppermute | solution.py:68
  132.2 4.2 %collective-permute-done.3 = f32[32,512]{1,0:T(8,128)S(1)} collective-permute-done((f32[32,512]{1,0:T(8,128)S(1)}, f32[32,512]{1,0:T(8,128)S(1)}, u32[]{:S(2)}, u32[]{:S(2)}) %collective-permute-start.3) | collective-permute-done | bytes 65568 | tf_op jit(solution)/shard_map/ppermute | solution.py:68
  136.5 0.7 collective-permute-start.4
  137.1 4.7 %collective-permute-done.4 = f32[16,512]{1,0:T(8,128)S(1)} collective-permute-done((f32[16,512]{1,0:T(8,128)S(1)}, f32[16,512]{1,0:T(8,128)S(1)}, u32[]{:S(2)}, u32[]{:S(2)}) %collective-permute-start.4) | collective-permute-done | bytes 32800 | tf_op jit(solution)/shard_map/ppermute | solution.py:68
  142.3 4.4 %collective-permute-done.5 = f32[16,512]{1,0:T(8,128)S(1)} collective-permute-done((f32[16,512]{1,0:T(8,128)S(1)}, f32[16,512]{1,0:T(8,128)S(1)}, u32[]{:S(2)}, u32[]{:S(2)}) %collective-permute-start.5) | collective-permute-done | bytes 32800 | tf_op jit(solution)/shard_map/ppermute | solution.py:71
  147.1 6.3 %collective-permute-done.6 = f32[32,512]{0,1:T(8,128)S(1)} collective-permute-done((f32[32,512]{0,1:T(8,128)S(1)}, f32[32,512]{0,1:T(8,128)S(1)}, u32[]{:S(2)}, u32[]{:S(2)}) %collective-permute-start.6) | collective-permute-done | bytes 65568 | tf_op jit(solution)/shard_map/ppermute | solution.py:71
  153.6 1.3 collective-permute-start.7
  154.9 5.1 %collective-permute-done.7 = f32[64,512]{0,1:T(8,128)S(1)} collective-permute-done((f32[64,512]{0,1:T(8,128)S(1)}, f32[64,512]{0,1:T(8,128)S(1)}, u32[]{:S(2)}, u32[]{:S(2)}) %collective-permute-start.7) | collective-permute-done | bytes 131104 | tf_op jit(solution)/shard_map/ppermute | solution.py:71
  160.3 1.4 collective-permute-start.8
  161.6 5.1 %collective-permute-done.8 = f32[128,512]{0,1:T(8,128)S(1)} collective-permute-done((f32[128,512]{0,1:T(8,128)S(1)}, f32[128,512]{0,1:T(8,128)S(1)}, u32[]{:S(2)}, u32[]{:S(2)}) %collective-permute-start.8) | collective-permute-done | bytes 262176 | tf_op jit(solution)/shard_map/ppermute | solution.py:71
  167.0 1.9 collective-permute-done.9
  169.2 11.7 %custom-call.12 = f32[128,128]{1,0:T(8,128)S(1)} custom-call(f32[128,128]{1,0:T(8,128)S(1)} %copy.97), custom_call_target="Cholesky" | custom-call | tf_op jit(solution)/shard_map/cholesky/custom-call.1 | solution.py:15
  181.6 0.7 select_bitcast_fusion.3
  182.2 9.8 %custom-call.13 = f32[1,128,128]{1,2,0:T(8,128)S(1)} custom-call(f32[1,128,128]{2,1,0:T(8,128)S(1)} %get-tuple-element.18), custom_call_target="InvertDiagBlocksLowerTriangular" | custom-call | tf_op jit(solution)/shard_map/triangular_solve/custom-call.0 | solution.py:17
  192.7 0.7 fusion.27
  194.5 11.9 %custom-call.14 = f32[128,128]{1,0:T(8,128)S(1)} custom-call(f32[128,128]{1,0:T(8,128)S(1)} %copy.101), custom_call_target="Cholesky" | custom-call | tf_op jit(solution)/shard_map/cholesky/custom-call.1 | solution.py:15
  207.7 9.8 %custom-call.15 = f32[1,128,128]{1,2,0:T(8,128)S(1)} custom-call(f32[1,128,128]{2,1,0:T(8,128)S(1)} %get-tuple-element.16), custom_call_target="InvertDiagBlocksLowerTriangular" | custom-call | tf_op jit(solution)/shard_map/triangular_solve/custom-call.0 | solution.py:17
  218.8 11.7 %custom-call.16 = f32[128,128]{1,0:T(8,128)S(1)} custom-call(f32[128,128]{1,0:T(8,128)S(1)} %fusion.46), custom_call_target="Cholesky" | custom-call | tf_op jit(solution)/shard_map/cholesky/custom-call.1 | solution.py:15
  231.8 9.8 %custom-call.17 = f32[1,128,128]{1,2,0:T(8,128)S(1)} custom-call(f32[1,128,128]{2,1,0:T(8,128)S(1)} %get-tuple-element.14), custom_call_target="InvertDiagBlocksLowerTriangular" | custom-call | tf_op jit(solution)/shard_map/triangular_solve/custom-call.0 | solution.py:17
  245.5 11.7 %custom-call.18 = f32[128,128]{1,0:T(8,128)S(1)} custom-call(f32[128,128]{1,0:T(8,128)S(1)} %broadcast_multiply_fusion), custom_call_target="Cholesky" | custom-call | tf_op jit(solution)/shard_map/cholesky/custom-call.1 | solution.py:15
  258.6 9.8 %custom-call.19 = f32[1,128,128]{1,2,0:T(8,128)S(1)} custom-call(f32[1,128,128]{2,1,0:T(8,128)S(1)} %get-tuple-element.12), custom_call_target="InvertDiagBlocksLowerTriangular" | custom-call | tf_op jit(solution)/shard_map/triangular_solve/custom-call.0 | solution.py:17
  270.5 10.0 %multiply_bitcast_fusion = f32[2048,512]{0,1:T(8,128)} fusion(f32[512,2048]{1,0:T(8,128)} %bitcast.1, f32[128,256]{1,0:T(8,128)S(1)} %broadcast.51, f32[128,128]{1,0:T(8,128)S(1)} %broadcast.64, f32[128,128]{1,0:T(8,128)S(1)} %fusion.38, f32[128,128]{1,0:T(8,128)S(1)} %copy.120, f32[128,128]{1,0:T(8,128)S(1)} %convolution_negate_fusion, ...), kind=kOutput, calls=%fused_computation.1 | convolution fusion | flops 6446907392 | bytes 9240576 | tf_op jit(solution)/shard_map/dot_general | solution.py:92
  280.6 5.3 %copy.122 = f32[2048,512]{1,0:T(8,128)} copy(f32[2048,512]{0,1:T(8,128)} %multiply_bitcast_fusion) | data formatting | bytes 8388608
  286.2 1.3 copy.123
  (90 shorter events, 15.7 us)
Async XLA Ops:
  5.3 101.3 %all-to-all-start = ((f32[16,32,2048]{2,0,1:T(8,128)}), f32[16,32,2048]{2,0,1:T(8,128)}, u32[]{:S(2)}, u32[]{:S(2)}) async-start(f32[16,32,2048]{2,0,1:T(8,128)} %bitcast.82), calls=%async_computation | async-start | bytes 8388608 | tf_op jit(solution)/shard_map/all_to_all | solution.py:82
  116.5 2.0 collective-permute-start
  118.6 8.4 %collective-permute-start.1 = (f32[128,512]{1,0:T(8,128)S(1)}, f32[128,512]{1,0:T(8,128)S(1)}, u32[]{:S(2)}, u32[]{:S(2)}) collective-permute-start(f32[128,512]{1,0:T(8,128)S(1)} %constant_dynamic-slice_fusion.3), channel_id=1, source_target_pairs={{0,2},{1,3},{2,0},{3,1},{4,6},{5,7},{6,4},{7,5},{8,10},{9,11},{10,... | collective-permute-start | bytes 786440 | tf_op jit(solution)/shard_map/ppermute | solution.py:68
  127.0 5.0 %collective-permute-start.2 = (f32[64,512]{1,0:T(8,128)S(1)}, f32[64,512]{1,0:T(8,128)S(1)}, u32[]{:S(2)}, u32[]{:S(2)}) collective-permute-start(f32[64,512]{1,0:T(8,128)S(1)} %constant_dynamic-slice_fusion.2), channel_id=1, source_target_pairs={{0,4},{1,5},{2,6},{3,7},{4,0},{5,1},{6,2},{7,3},{8,12},{9,13},{10,... | collective-permute-start | bytes 393224 | tf_op jit(solution)/shard_map/ppermute | solution.py:68
  132.1 4.3 %collective-permute-start.3 = (f32[32,512]{1,0:T(8,128)S(1)}, f32[32,512]{1,0:T(8,128)S(1)}, u32[]{:S(2)}, u32[]{:S(2)}) collective-permute-start(f32[32,512]{1,0:T(8,128)S(1)} %constant_dynamic-slice_fusion.1), channel_id=1, source_target_pairs={{0,8},{1,9},{2,10},{3,11},{4,12},{5,13},{6,14},{7,15},{8,0},{9,1},... | collective-permute-start | bytes 196616 | tf_op jit(solution)/shard_map/ppermute | solution.py:68
  136.5 5.4 %collective-permute-start.4 = (f32[16,512]{1,0:T(8,128)S(1)}, f32[16,512]{1,0:T(8,128)S(1)}, u32[]{:S(2)}, u32[]{:S(2)}) collective-permute-start(f32[16,512]{1,0:T(8,128)S(1)} %constant_dynamic-slice_fusion), channel_id=1, source_target_pairs={{0,16},{1,17},{2,18},{3,19},{4,20},{5,21},{6,22},{7,23},{8,24},{9,... | collective-permute-start | bytes 98312 | tf_op jit(solution)/shard_map/ppermute | solution.py:68
  141.9 4.9 %collective-permute-start.5 = (f32[16,512]{1,0:T(8,128)S(1)}, f32[16,512]{1,0:T(8,128)S(1)}, u32[]{:S(2)}, u32[]{:S(2)}) collective-permute-start(f32[16,512]{1,0:T(8,128)S(1)} %dynamic-slice_add_fusion.4), channel_id=1, source_target_pairs={{0,16},{1,17},{2,18},{3,19},{4,20},{5,21},{6,22},{7,23},{8,24},{9,... | collective-permute-start | bytes 98312 | tf_op jit(solution)/shard_map/ppermute | solution.py:71
  146.9 6.4 %collective-permute-start.6 = (f32[32,512]{0,1:T(8,128)S(1)}, f32[32,512]{0,1:T(8,128)S(1)}, u32[]{:S(2)}, u32[]{:S(2)}) collective-permute-start(f32[32,512]{0,1:T(8,128)S(1)} %copy.93), channel_id=1, source_target_pairs={{0,8},{1,9},{2,10},{3,11},{4,12},{5,13},{6,14},{7,15},{8,0},{9,1},... | collective-permute-start | bytes 196616 | tf_op jit(solution)/shard_map/ppermute | solution.py:71
  153.6 6.4 %collective-permute-start.7 = (f32[64,512]{0,1:T(8,128)S(1)}, f32[64,512]{0,1:T(8,128)S(1)}, u32[]{:S(2)}, u32[]{:S(2)}) collective-permute-start(f32[64,512]{0,1:T(8,128)S(1)} %pad_maximum_fusion.6), channel_id=1, source_target_pairs={{0,4},{1,5},{2,6},{3,7},{4,0},{5,1},{6,2},{7,3},{8,12},{9,13},{10,... | collective-permute-start | bytes 393224 | tf_op jit(solution)/shard_map/ppermute | solution.py:71
  160.3 6.4 %collective-permute-start.8 = (f32[128,512]{0,1:T(8,128)S(1)}, f32[128,512]{0,1:T(8,128)S(1)}, u32[]{:S(2)}, u32[]{:S(2)}) collective-permute-start(f32[128,512]{0,1:T(8,128)S(1)} %pad_maximum_fusion.7), channel_id=1, source_target_pairs={{0,2},{1,3},{2,0},{3,1},{4,6},{5,7},{6,4},{7,5},{8,10},{9,11},{10,... | collective-permute-start | bytes 786440 | tf_op jit(solution)/shard_map/ppermute | solution.py:71
  166.9 2.0 collective-permute-start.9
where the time goes:
time: 292 us; the launch traced here: 288 us
  waiting for transfers between devices  138 us (47%)
  other arithmetic  92.6 us (32%)
  matrix products  28 us (10%)
  starting transfers between devices  14.2 us (5%)
  local copies, waits for them, and re-layouts  13.1 us (4%)
    all_to_all x1, waiting for transfers between devices, per_device(): lax.all_to_all(sample_t, AXES, split_axis=1, concat_axis=0, tiled=True)  93.9 us
    another operation x12, other arithmetic, _diag_pair(): lower = lax.linalg.cholesky(block)  49.7 us
    another operation x8, other arithmetic, _diag_pair(): lax.linalg.triangular_solve(lower, identity, left_side=True, lower=True)  41.9 us
    ppermute x5, waiting for transfers between devices, sum_by_halving(): recv = lax.ppermute(buf, AXES, _pair(count, 1 << k))  22.8 us
    ppermute x5, waiting for transfers between devices, sum_by_halving(): buf = keep + lax.ppermute(send, AXES, _pair(count, 1 << k))  21.6 us
    dot_general x1, matrix products, per_device(): lax.dot_general(rows_t, inverse, (((0,), (0,)), ((), ())), precision=lax....  10 us
    dot_general x1, matrix products, per_device(): jnp.dot(rows_t, rows_t.T, precision=lax.Precision.HIGHEST, preferred_elem...  9.77 us
    all_to_all x1, starting transfers between devices, per_device(): lax.all_to_all(sample_t, AXES, split_axis=1, concat_axis=0, tiled=True)  7.43 us
  transfers between devices with their start and end apart: 11, of which 11 were waited for; matrix products, arithmetic and copies ran while one was open for 0% of the time, Pallas kernels for 0%

commit v1 on v0

--- a/solution.py
+++ b/solution.py
@@ -79,7 +79,10 @@
     wide_count = lax.axis_size("wide")
     narrow_count = lax.axis_size("narrow")
     count = wide_count * narrow_count
-    rows_t = lax.all_to_all(sample_t, AXES, split_axis=1, concat_axis=0, tiled=True)
+    rows_t = jnp.concatenate(
+        lax.all_to_all(jnp.stack(jnp.split(sample_t, lax.axis_size(AXES), axis=1)), AXES, 0, 0),
+        axis=0,
+    )
     gram_local = jnp.dot(
         rows_t, rows_t.T, precision=lax.Precision.HIGHEST, preferred_element_type=jnp.float32
     )

time: 292 us -> 339 us (1.16)
  local copies, waits for them, and re-layouts: 13.1 us -> 53.2 us
  matrix products: 28 us -> 34.5 us
    unnamed x9 -> x39, local copies, waits for them, and re-layouts: 7.13 us -> 50.4 us
    dot_general x1, matrix products: 10 us -> 16.5 us  [per_device(): lax.dot_general(rows_t, inverse, (((0,), (0,)), ((), ())), precision=lax....]
    all_to_all x1 -> x0, local copies, waits for them, and re-layouts: 4.7 us -> none  [per_device(): lax.all_to_all(sample_t, AXES, split_axis=1, concat_axis=0, tiled=True)]
where the time goes in v1:
time: 339 us; the launch traced here: 334 us
  waiting for transfers between devices  138 us (41%)
  other arithmetic  92.6 us (27%)
  local copies, waits for them, and re-layouts  53.2 us (16%)
  matrix products  34.5 us (10%)
  starting transfers between devices  14.2 us (4%)
    all_to_all x1, waiting for transfers between devices, per_device(): lax.all_to_all(jnp.stack(jnp.split(sample_t, lax.axis_size(AXES), axis=1)...  93.9 us
    unnamed x39, local copies, waits for them, and re-layouts  50.4 us
    another operation x12, other arithmetic, _diag_pair(): lower = lax.linalg.cholesky(block)  49.7 us
    another operation x8, other arithmetic, _diag_pair(): lax.linalg.triangular_solve(lower, identity, left_side=True, lower=True)  41.9 us
    ppermute x5, waiting for transfers between devices, sum_by_halving(): recv = lax.ppermute(buf, AXES, _pair(count, 1 << k))  22.8 us
    ppermute x5, waiting for transfers between devices, sum_by_halving(): buf = keep + lax.ppermute(send, AXES, _pair(count, 1 << k))  21.7 us
    dot_general x1, matrix products, per_device(): lax.dot_general(rows_t, inverse, (((0,), (0,)), ((), ())), precision=lax....  16.5 us
    dot_general x1, matrix products, per_device(): jnp.dot(rows_t, rows_t.T, precision=lax.Precision.HIGHEST, preferred_elem...  9.83 us
  transfers between devices with their start and end apart: 11, of which 11 were waited for; matrix products, arithmetic and copies ran while one was open for 0% of the time, Pallas kernels for 0%

profile of v1, /device:TPU:0, one launch (start us, length us, event | category | flops | bytes accessed | tf_op | source)
XLA Modules:
  0.0 334.4 jit_solution(11222898714630203223)
XLA Ops:
  0.6 1.6 bitcast_dynamic-update-slice_fusion.31
  3.8 1.6 bitcast_dynamic-update-slice_fusion.29
  5.3 1.6 bitcast_dynamic-update-slice_fusion.28
  10.0 1.6 bitcast_dynamic-update-slice_fusion.25
  11.6 1.6 bitcast_dynamic-update-slice_fusion.24
  16.3 1.6 bitcast_dynamic-update-slice_fusion.21
  22.6 1.6 bitcast_dynamic-update-slice_fusion.17
  27.3 1.6 bitcast_dynamic-update-slice_fusion.14
  28.9 1.6 bitcast_dynamic-update-slice_fusion.13
  33.6 1.6 bitcast_dynamic-update-slice_fusion.10
  50.8 7.4 %all-to-all-start = ((f32[32,16,2048]{2,1,0:T(8,128)}), f32[32,16,2048]{2,1,0:T(8,128)}, u32[]{:S(2)}, u32[]{:S(2)}) async-start(f32[32,16,2048]{2,1,0:T(8,128)} %bitcast_dynamic-update-slice_fusion), calls=%async_computation | async-start | bytes 8388608 | tf_op jit(solution)/shard_map/all_to_all | solution.py:83
  58.2 93.9 %all-to-all-done = f32[32,16,2048]{2,1,0:T(8,128)} async-done(((f32[32,16,2048]{2,1,0:T(8,128)}), f32[32,16,2048]{2,1,0:T(8,128)}, u32[]{:S(2)}, u32[]{:S(2)}) %all-to-all-start) | async-done | bytes 4194336 | tf_op jit(solution)/shard_map/all_to_all | solution.py:83
  152.1 9.8 %fusion.71 = f32[512,512]{1,0:T(8,128)S(1)} fusion(f32[512,2048]{1,0:T(8,128)} %bitcast.32), kind=kOutput, calls=%fused_computation.168 | convolution fusion | flops 6442450944 | bytes 5242880 | tf_op jit(solution)/shard_map/dot_general | solution.py:86
  162.1 1.9 collective-permute-done
  165.4 7.1 %collective-permute-done.1 = f32[128,512]{1,0:T(8,128)S(1)} collective-permute-done((f32[128,512]{1,0:T(8,128)S(1)}, f32[128,512]{1,0:T(8,128)S(1)}, u32[]{:S(2)}, u32[]{:S(2)}) %collective-permute-start.1) | collective-permute-done | bytes 262176 | tf_op jit(solution)/shard_map/ppermute | solution.py:68
  173.9 3.7 %collective-permute-done.2 = f32[64,512]{1,0:T(8,128)S(1)} collective-permute-done((f32[64,512]{1,0:T(8,128)S(1)}, f32[64,512]{1,0:T(8,128)S(1)}, u32[]{:S(2)}, u32[]{:S(2)}) %collective-permute-start.2) | collective-permute-done | bytes 131104 | tf_op jit(solution)/shard_map/ppermute | solution.py:68
  177.7 4.2 %collective-permute-done.3 = f32[32,512]{1,0:T(8,128)S(1)} collective-permute-done((f32[32,512]{1,0:T(8,128)S(1)}, f32[32,512]{1,0:T(8,128)S(1)}, u32[]{:S(2)}, u32[]{:S(2)}) %collective-permute-start.3) | collective-permute-done | bytes 65568 | tf_op jit(solution)/shard_map/ppermute | solution.py:68
  182.7 4.7 %collective-permute-done.4 = f32[16,512]{1,0:T(8,128)S(1)} collective-permute-done((f32[16,512]{1,0:T(8,128)S(1)}, f32[16,512]{1,0:T(8,128)S(1)}, u32[]{:S(2)}, u32[]{:S(2)}) %collective-permute-start.4) | collective-permute-done | bytes 32800 | tf_op jit(solution)/shard_map/ppermute | solution.py:68
  187.9 4.4 %collective-permute-done.5 = f32[16,512]{1,0:T(8,128)S(1)} collective-permute-done((f32[16,512]{1,0:T(8,128)S(1)}, f32[16,512]{1,0:T(8,128)S(1)}, u32[]{:S(2)}, u32[]{:S(2)}) %collective-permute-start.5) | collective-permute-done | bytes 32800 | tf_op jit(solution)/shard_map/ppermute | solution.py:71
  192.6 6.3 %collective-permute-done.6 = f32[32,512]{0,1:T(8,128)S(1)} collective-permute-done((f32[32,512]{0,1:T(8,128)S(1)}, f32[32,512]{0,1:T(8,128)S(1)}, u32[]{:S(2)}, u32[]{:S(2)}) %collective-permute-start.6) | collective-permute-done | bytes 65568 | tf_op jit(solution)/shard_map/ppermute | solution.py:71
  200.4 5.1 %collective-permute-done.7 = f32[64,512]{0,1:T(8,128)S(1)} collective-permute-done((f32[64,512]{0,1:T(8,128)S(1)}, f32[64,512]{0,1:T(8,128)S(1)}, u32[]{:S(2)}, u32[]{:S(2)}) %collective-permute-start.7) | collective-permute-done | bytes 131104 | tf_op jit(solution)/shard_map/ppermute | solution.py:71
  207.2 5.1 %collective-permute-done.8 = f32[128,512]{0,1:T(8,128)S(1)} collective-permute-done((f32[128,512]{0,1:T(8,128)S(1)}, f32[128,512]{0,1:T(8,128)S(1)}, u32[]{:S(2)}, u32[]{:S(2)}) %collective-permute-start.8) | collective-permute-done | bytes 262176 | tf_op jit(solution)/shard_map/ppermute | solution.py:71
  212.5 1.9 collective-permute-done.9
  214.7 11.7 %custom-call.12 = f32[128,128]{1,0:T(8,128)S(1)} custom-call(f32[128,128]{1,0:T(8,128)S(1)} %copy.35), custom_call_target="Cholesky" | custom-call | tf_op jit(solution)/shard_map/cholesky/custom-call.1 | solution.py:15
  227.8 9.8 %custom-call.13 = f32[1,128,128]{1,2,0:T(8,128)S(1)} custom-call(f32[1,128,128]{2,1,0:T(8,128)S(1)} %get-tuple-element.14), custom_call_target="InvertDiagBlocksLowerTriangular" | custom-call | tf_op jit(solution)/shard_map/triangular_solve/custom-call.0 | solution.py:17
  240.0 11.9 %custom-call.14 = f32[128,128]{1,0:T(8,128)S(1)} custom-call(f32[128,128]{1,0:T(8,128)S(1)} %copy.39), custom_call_target="Cholesky" | custom-call | tf_op jit(solution)/shard_map/cholesky/custom-call.1 | solution.py:15
  253.2 9.8 %custom-call.15 = f32[1,128,128]{1,2,0:T(8,128)S(1)} custom-call(f32[1,128,128]{2,1,0:T(8,128)S(1)} %get-tuple-element.12), custom_call_target="InvertDiagBlocksLowerTriangular" | custom-call | tf_op jit(solution)/shard_map/triangular_solve/custom-call.0 | solution.py:17
  264.3 11.7 %custom-call.16 = f32[128,128]{1,0:T(8,128)S(1)} custom-call(f32[128,128]{1,0:T(8,128)S(1)} %fusion.46), custom_call_target="Cholesky" | custom-call | tf_op jit(solution)/shard_map/cholesky/custom-call.1 | solution.py:15
  277.4 9.8 %custom-call.17 = f32[1,128,128]{1,2,0:T(8,128)S(1)} custom-call(f32[1,128,128]{2,1,0:T(8,128)S(1)} %get-tuple-element.10), custom_call_target="InvertDiagBlocksLowerTriangular" | custom-call | tf_op jit(solution)/shard_map/triangular_solve/custom-call.0 | solution.py:17
  291.0 11.7 %custom-call.18 = f32[128,128]{1,0:T(8,128)S(1)} custom-call(f32[128,128]{1,0:T(8,128)S(1)} %broadcast_multiply_fusion), custom_call_target="Cholesky" | custom-call | tf_op jit(solution)/shard_map/cholesky/custom-call.1 | solution.py:15
  304.1 9.8 %custom-call.19 = f32[1,128,128]{1,2,0:T(8,128)S(1)} custom-call(f32[1,128,128]{2,1,0:T(8,128)S(1)} %get-tuple-element.8), custom_call_target="InvertDiagBlocksLowerTriangular" | custom-call | tf_op jit(solution)/shard_map/triangular_solve/custom-call.0 | solution.py:17
  317.7 16.5 %convolution_multiply_fusion = f32[2048,512]{1,0:T(8,128)} fusion(f32[512,2048]{1,0:T(8,128)} %bitcast.32, f32[128,256]{1,0:T(8,128)S(1)} %broadcast.49, f32[128,128]{1,0:T(8,128)S(1)} %broadcast.62, f32[128,128]{1,0:T(8,128)S(1)} %fusion.38, f32[128,128]{1,0:T(8,128)S(1)} %copy.55, f32[128,128]{1,0:T(8,128)S(1)} %convolution_negate_fusion, ...), kind=kOutput, calls=%fused_computation | convolution fusion | flops 6446907392 | bytes 9240576 | tf_op jit(solution)/shard_map/dot_general | solution.py:95
  (120 shorter events, 58.8 us)
Async XLA Ops:
  50.8 101.3 %all-to-all-start = ((f32[32,16,2048]{2,1,0:T(8,128)}), f32[32,16,2048]{2,1,0:T(8,128)}, u32[]{:S(2)}, u32[]{:S(2)}) async-start(f32[32,16,2048]{2,1,0:T(8,128)} %bitcast_dynamic-update-slice_fusion), calls=%async_computation | async-start | bytes 8388608 | tf_op jit(solution)/shard_map/all_to_all | solution.py:83
  162.0 2.0 collective-permute-start
  164.1 8.4 %collective-permute-start.1 = (f32[128,512]{1,0:T(8,128)S(1)}, f32[128,512]{1,0:T(8,128)S(1)}, u32[]{:S(2)}, u32[]{:S(2)}) collective-permute-start(f32[128,512]{1,0:T(8,128)S(1)} %constant_dynamic-slice_fusion.3), channel_id=1, source_target_pairs={{0,2},{1,3},{2,0},{3,1},{4,6},{5,7},{6,4},{7,5},{8,10},{9,11},{10,... | collective-permute-start | bytes 786440 | tf_op jit(solution)/shard_map/ppermute | solution.py:68
  172.6 5.0 %collective-permute-start.2 = (f32[64,512]{1,0:T(8,128)S(1)}, f32[64,512]{1,0:T(8,128)S(1)}, u32[]{:S(2)}, u32[]{:S(2)}) collective-permute-start(f32[64,512]{1,0:T(8,128)S(1)} %constant_dynamic-slice_fusion.2), channel_id=1, source_target_pairs={{0,4},{1,5},{2,6},{3,7},{4,0},{5,1},{6,2},{7,3},{8,12},{9,13},{10,... | collective-permute-start | bytes 393224 | tf_op jit(solution)/shard_map/ppermute | solution.py:68
  177.7 4.3 %collective-permute-start.3 = (f32[32,512]{1,0:T(8,128)S(1)}, f32[32,512]{1,0:T(8,128)S(1)}, u32[]{:S(2)}, u32[]{:S(2)}) collective-permute-start(f32[32,512]{1,0:T(8,128)S(1)} %constant_dynamic-slice_fusion.1), channel_id=1, source_target_pairs={{0,8},{1,9},{2,10},{3,11},{4,12},{5,13},{6,14},{7,15},{8,0},{9,1},... | collective-permute-start | bytes 196616 | tf_op jit(solution)/shard_map/ppermute | solution.py:68
  182.0 5.4 %collective-permute-start.4 = (f32[16,512]{1,0:T(8,128)S(1)}, f32[16,512]{1,0:T(8,128)S(1)}, u32[]{:S(2)}, u32[]{:S(2)}) collective-permute-start(f32[16,512]{1,0:T(8,128)S(1)} %constant_dynamic-slice_fusion), channel_id=1, source_target_pairs={{0,16},{1,17},{2,18},{3,19},{4,20},{5,21},{6,22},{7,23},{8,24},{9,... | collective-permute-start | bytes 98312 | tf_op jit(solution)/shard_map/ppermute | solution.py:68
  187.4 4.9 %collective-permute-start.5 = (f32[16,512]{1,0:T(8,128)S(1)}, f32[16,512]{1,0:T(8,128)S(1)}, u32[]{:S(2)}, u32[]{:S(2)}) collective-permute-start(f32[16,512]{1,0:T(8,128)S(1)} %dynamic-slice_add_fusion.4), channel_id=1, source_target_pairs={{0,16},{1,17},{2,18},{3,19},{4,20},{5,21},{6,22},{7,23},{8,24},{9,... | collective-permute-start | bytes 98312 | tf_op jit(solution)/shard_map/ppermute | solution.py:71
  192.5 6.4 %collective-permute-start.6 = (f32[32,512]{0,1:T(8,128)S(1)}, f32[32,512]{0,1:T(8,128)S(1)}, u32[]{:S(2)}, u32[]{:S(2)}) collective-permute-start(f32[32,512]{0,1:T(8,128)S(1)} %copy.31), channel_id=1, source_target_pairs={{0,8},{1,9},{2,10},{3,11},{4,12},{5,13},{6,14},{7,15},{8,0},{9,1},... | collective-permute-start | bytes 196616 | tf_op jit(solution)/shard_map/ppermute | solution.py:71
  199.1 6.4 %collective-permute-start.7 = (f32[64,512]{0,1:T(8,128)S(1)}, f32[64,512]{0,1:T(8,128)S(1)}, u32[]{:S(2)}, u32[]{:S(2)}) collective-permute-start(f32[64,512]{0,1:T(8,128)S(1)} %pad_maximum_fusion.6), channel_id=1, source_target_pairs={{0,4},{1,5},{2,6},{3,7},{4,0},{5,1},{6,2},{7,3},{8,12},{9,13},{10,... | collective-permute-start | bytes 393224 | tf_op jit(solution)/shard_map/ppermute | solution.py:71
  205.8 6.4 %collective-permute-start.8 = (f32[128,512]{0,1:T(8,128)S(1)}, f32[128,512]{0,1:T(8,128)S(1)}, u32[]{:S(2)}, u32[]{:S(2)}) collective-permute-start(f32[128,512]{0,1:T(8,128)S(1)} %pad_maximum_fusion.7), channel_id=1, source_target_pairs={{0,2},{1,3},{2,0},{3,1},{4,6},{5,7},{6,4},{7,5},{8,10},{9,11},{10,... | collective-permute-start | bytes 786440 | tf_op jit(solution)/shard_map/ppermute | solution.py:71
  212.4 2.0 collective-permute-start.9
